TPU v7x, 128 devices: a whole 4x4x4 slice. The times are simulated.
128 devices in a mesh: req: 16 (over y, x), kv: 8 (over z, core).
Axes of the slice: x: 4, y: 4, z: 4, core: 2. Of those that a mesh axis runs over, the one named last changes fastest.
Arguments:
- hidden: bfloat16 [1024, 1536], P('req', 'kv'), may hold values from -6 to 6
- perm: int32 [1024], replicated, may hold values from 0 to 1023, as said below
- seq_lens: int32 [1024], P('req'), may hold values from 1 to 4096, as said below
- page_table: int32 [1024, 32], P('req'), may hold values from 0 to 319, as said below
- kv_cache: bfloat16 [5120, 8, 128, 128], P('req', 'kv'), may hold values from -52 to 52
- attn_gain: float32 [1536], replicated, may hold values from 0.1 to 1.9
- qkv_weight: bfloat16 [8, 1536, 320], P('kv'), may hold values from -0.15625 to 0.15625
- out_weight: bfloat16 [8, 192, 1536], P('kv'), may hold values from -1 to 1
- ffn_gain: float32 [1536], replicated, may hold values from 0.1 to 1.9
- router: bfloat16 [1536, 16], replicated, may hold values from -0.15625 to 0.15625
- routes: int32 [1024, 2], P(('req', 'kv')), may hold values from 0 to 15, all different within a row; in each aligned block of 8 rows (0 to 7, 8 to 15, ...) at most 2 rows name the same one
- gate_up: bfloat16 [16, 1536, 2048], P('req'), may hold values from -0.15625 to 0.15625
- down: bfloat16 [16, 1024, 1536], P('req'), may hold values from -0.1875 to 0.1875
Outputs:
- mixed: bfloat16 [1024, 1536], P(('req', 'kv'))
Inputs may be any that keep to these rules, and one draw needn't show every extreme that they name: A permutation of the 1024 requests: slot s holds request perm[s]. The 64 slots of each index of req hold exactly 4 requests from each block of 64 consecutive requests. `seq_lens`: the length 4096 is reached on every index of req. `page_table`: entries 0 to (seq_lens[s] + 127) // 128 - 1 of row s are used; no page of one index of req is used by two of its slots; later entries name arbitrary pages.
All inputs are finite; a program needn't handle non-finite values.
Results may differ from a plain program's by a relative error of at most 0.017.
Values may be sent and summed in bfloat16 or wider, within the bound.
No kernel may reach another device: no remote copies, remote signals or barrier semaphores. Data moves between devices by JAX's collectives and lax.ppermute only.
A program may use at most 128 MiB of HBM per device.

v0:
```python
import jax
import jax.numpy as jnp
from jax import lax
from jax.sharding import PartitionSpec as P

REQ_DEV = 64
NEG_FILL = -1e30
EPS_NORM = 1e-05


def rms_norm(values, gain_vec):
    values = values.astype(jnp.float32)
    factor = lax.rsqrt(jnp.mean(values * values, axis=-1, keepdims=True) + EPS_NORM)
    return (values * factor * gain_vec).astype(jnp.bfloat16)


def attend(normed, seq_lens, page_table, kv_cache, qkv_weight):
    pool_pages, local_heads, twice_hd, page_len = kv_cache.shape
    head_dim = twice_hd // 2
    slot_count = normed.shape[0]
    groups = qkv_weight.shape[2] // head_dim - 2
    max_pages = page_table.shape[1]
    projected = jnp.einsum("sd,hdc->shc", normed, qkv_weight, preferred_element_type=jnp.float32)
    queries = (
        projected[:, :, : groups * head_dim]
        .reshape(slot_count, local_heads, groups, head_dim)
        .astype(jnp.bfloat16)
    )
    key_new = projected[:, :, groups * head_dim : (groups + 1) * head_dim].astype(jnp.bfloat16)
    value_new = projected[:, :, (groups + 1) * head_dim :].astype(jnp.bfloat16)
    page_need = (seq_lens + page_len - 1) // page_len
    page_ids = jnp.arange(max_pages, dtype=jnp.int32)
    in_use = page_ids[None, :] < page_need[:, None]
    target_page = jnp.where(in_use, page_table, pool_pages).reshape(-1)
    slot_ids = jnp.broadcast_to(
        jnp.arange(slot_count, dtype=jnp.int32)[:, None], (slot_count, max_pages)
    ).reshape(-1)
    order_ids = jnp.broadcast_to(page_ids[None, :], (slot_count, max_pages)).reshape(-1)
    owner = (
        jnp.full((pool_pages,), slot_count, jnp.int32).at[target_page].set(slot_ids, mode="drop")
    )
    page_order = jnp.zeros((pool_pages,), jnp.int32).at[target_page].set(order_ids, mode="drop")
    owner_safe = jnp.minimum(owner, slot_count - 1)
    position = page_order[:, None] * page_len + jnp.arange(page_len, dtype=jnp.int32)[None, :]
    live = (owner[:, None] < slot_count) & (position < jnp.take(seq_lens, owner_safe)[:, None])
    scale_factor = head_dim ** (-0.5)
    page_queries = jnp.take(queries, owner_safe, axis=0)
    scores = (
        jnp.einsum(
            "pkgd,pkdt->pkgt",
            page_queries,
            kv_cache[:, :, :head_dim, :],
            preferred_element_type=jnp.float32,
        )
        * scale_factor
    )
    scores = jnp.where(live[:, None, None, :], scores, NEG_FILL)
    score_new = (
        jnp.einsum("skgd,skd->skg", queries, key_new, preferred_element_type=jnp.float32)
        * scale_factor
    )
    page_peak = jnp.max(scores, axis=3)
    belongs = owner[None, :] == jnp.arange(slot_count, dtype=jnp.int32)[:, None]
    slot_peak = jnp.max(jnp.where(belongs[:, :, None, None], page_peak[None], NEG_FILL), axis=1)
    slot_peak = jnp.maximum(slot_peak, score_new)
    weights = jnp.where(
        live[:, None, None, :],
        jnp.exp(scores - jnp.take(slot_peak, owner_safe, axis=0)[..., None]),
        0.0,
    )
    page_total = jnp.sum(weights, axis=3)
    page_value = jnp.einsum(
        "pkgt,pkdt->pkgd",
        weights.astype(jnp.bfloat16),
        kv_cache[:, :, head_dim:, :],
        preferred_element_type=jnp.float32,
    )
    belongs_f = belongs.astype(jnp.float32)
    total_sum = jnp.dot(
        belongs_f, page_total.reshape(pool_pages, -1), precision=lax.Precision.HIGHEST
    ).reshape(slot_count, local_heads, groups)
    value_sum = jnp.dot(
        belongs_f, page_value.reshape(pool_pages, -1), precision=lax.Precision.HIGHEST
    ).reshape(slot_count, local_heads, groups, head_dim)
    weight_new = jnp.exp(score_new - slot_peak)
    total_sum = total_sum + weight_new
    rounded_new = lax.optimization_barrier(weight_new.astype(jnp.bfloat16)).astype(jnp.float32)
    value_sum = value_sum + rounded_new[..., None] * value_new.astype(jnp.float32)[:, :, None, :]
    return (value_sum / total_sum[..., None]).astype(jnp.bfloat16).reshape(slot_count, -1)


def expert_apply(piece, gate_up, down):
    n_source, slot_num, local_experts, width = piece.shape
    rows_in = piece.transpose(2, 0, 1, 3).reshape(local_experts, n_source * slot_num, width)
    projected_up = jnp.einsum("erd,edf->erf", rows_in, gate_up, preferred_element_type=jnp.float32)
    hidden_units = gate_up.shape[2] // 2
    acts = (
        jax.nn.silu(projected_up[..., :hidden_units]) * projected_up[..., hidden_units:]
    ).astype(jnp.bfloat16)
    result = jnp.einsum("erf,efd->erd", acts, down, preferred_element_type=jnp.float32).astype(
        jnp.bfloat16
    )
    return result.reshape(local_experts, n_source, slot_num, width).transpose(1, 2, 0, 3)


def shards(
    hidden,
    perm,
    seq_lens,
    page_table,
    kv_cache,
    attn_gain,
    qkv_weight,
    out_weight,
    ffn_gain,
    router,
    routes,
    gate_up,
    down,
):
    req_index = lax.axis_index("req")
    kv_index = lax.axis_index("kv")
    every_row = lax.all_gather(hidden, "req", axis=0, tiled=True)
    my_perm = lax.dynamic_slice_in_dim(perm, req_index * REQ_DEV, REQ_DEV)
    picked_rows = jnp.take(every_row, my_perm, axis=0)
    tokens = lax.all_gather(picked_rows, "kv", axis=1, tiled=True)
    normed = rms_norm(tokens, attn_gain)
    head_out = attend(normed, seq_lens, page_table, kv_cache, qkv_weight)
    sub_rows = routes.shape[0]
    width = tokens.shape[1]
    out_flat = out_weight.reshape(-1, out_weight.shape[2])
    attn_rows = lax.psum_scatter(
        jnp.dot(head_out, out_flat, preferred_element_type=jnp.float32).astype(jnp.bfloat16),
        "kv",
        scatter_dimension=0,
        tiled=True,
    ).astype(jnp.float32)
    own_tokens = lax.dynamic_slice_in_dim(tokens, kv_index * sub_rows, sub_rows, 0)
    residual = (own_tokens.astype(jnp.float32) + attn_rows).astype(jnp.bfloat16)
    normed_ffn = rms_norm(residual, ffn_gain)
    logits = jnp.dot(normed_ffn, router, preferred_element_type=jnp.float32)
    chosen = jnp.take_along_axis(logits, routes, axis=1)
    sigmoid_vals = jax.nn.sigmoid(chosen)
    gates = sigmoid_vals / jnp.sum(sigmoid_vals, axis=1, keepdims=True)
    experts_all = router.shape[1]
    n_req = lax.axis_size("req")
    local_experts = gate_up.shape[0]
    capacity = max(2, 2 * sub_rows // experts_all + 1)
    flat_routes = routes.reshape(-1)
    onehot_int = (flat_routes[:, None] == jnp.arange(experts_all, dtype=jnp.int32)[None, :]).astype(
        jnp.int32
    )
    earlier = jnp.cumsum(onehot_int, axis=0) - onehot_int
    rank_in = jnp.sum(earlier * onehot_int, axis=1)
    place_at = (
        flat_routes // local_experts * capacity * local_experts
        + rank_in * local_experts
        + flat_routes % local_experts
    )
    placement_plan = (
        place_at[:, None] == jnp.arange(experts_all * capacity, dtype=jnp.int32)[None, :]
    ).astype(jnp.bfloat16)
    paired_rows = jnp.repeat(normed_ffn, 2, axis=0)
    outgoing = jnp.einsum(
        "qe,qd->ed", placement_plan, paired_rows, preferred_element_type=jnp.float32
    )
    outgoing = outgoing.astype(jnp.bfloat16).reshape(n_req, capacity, local_experts, width)
    arrived = lax.all_to_all(outgoing, "req", split_axis=0, concat_axis=0, tiled=True)
    returned = lax.all_to_all(
        expert_apply(arrived, gate_up, down), "req", split_axis=0, concat_axis=0, tiled=True
    )
    back_rows = returned.reshape(experts_all * capacity, width)
    paired_output = jnp.dot(placement_plan, back_rows, preferred_element_type=jnp.float32).reshape(
        sub_rows, 2, width
    )
    mixed = residual.astype(jnp.float32) + jnp.sum(gates[:, :, None] * paired_output, axis=1)
    return mixed.astype(jnp.bfloat16)


def solution(mesh):
    in_specs = (
        P("req", "kv"),
        P(),
        P("req"),
        P("req", None),
        P("req", "kv", None, None),
        P(),
        P("kv", None, None),
        P("kv", None, None),
        P(),
        P(),
        P(("req", "kv"), None),
        P("req", None, None),
        P("req", None, None),
    )
    out_specs = P(("req", "kv"), None)
    return jax.shard_map(shards, mesh=mesh, in_specs=in_specs, out_specs=out_specs, check_vma=False)
```

profile of v0, /device:TPU:0, one launch (start us, length us, event | category | flops | bytes accessed | tf_op | source)
XLA Modules:
  0.0 223.6 jit_solution(11353303705725707446)
XLA Ops:
  6.5 2.1 fusion.66
  8.6 2.1 fusion.67
  10.7 2.1 fusion.68
  13.4 1.6 fusion.69
  16.0 8.0 %scatter_custom_fusion = s32[320]{0:T(512)S(1)} fusion(s32[2048]{0:T(1024)S(1)} %bitcast.180, s32[2048]{0:T(1024)S(1)} %reshape.468, s32[]{:T(128)} %constant.102.clone.1), kind=kCustom, calls=%fused_computation.112 | custom fusion | bytes 1284 | tf_op jit(solution)/shard_map/scatter | solution.py:40
  26.0 26.8 %all_gather.6 = bf16[1024,192]{1,0:T(8,128)(2,1)} all-gather(bf16[64,192]{1,0:T(8,128)(2,1)} %param.13), channel_id=1, replica_groups=mesh['req'=16,'kv'=8] {'req'}, dimensions={0}, use_global_device_ids=true | all-gather | bytes 417792 | tf_op jit(solution)/shard_map/all_gather | solution.py:123
  52.8 1.8 gather_fusion
  54.7 14.0 %all-gather = bf16[8,192,64]{1,2,0:T(8,128)(2,1)S(1)} all-gather(bf16[1,192,64]{1,2,0:T(8,128)(2,1)S(1)} %select_bitcast_fusion), channel_id=1, replica_groups=mesh['req'=16,'kv'=8] {'kv'}, dimensions={0}, use_global_device_ids=true | all-gather | bytes 221184 | tf_op jit(solution)/shard_map/all_gather | solution.py:126
  69.6 1.2 reshape.494
  70.9 1.7 convolution_bitcast_fusion
  73.3 8.2 %scatter_custom_fusion.1 = s32[320]{0:T(512)S(1)} fusion(s32[2048]{0:T(1024)S(1)} %bitcast.181, s32[2048]{0:T(1024)S(1)} %reshape.476, s32[]{:T(128)} %constant.106.clone.1), kind=kCustom, calls=%fused_computation.109 | custom fusion | bytes 1284 | tf_op jit(solution)/shard_map/scatter | solution.py:42
  83.1 2.5 %gather_fusion.1 = bf16[320,3,64]{2,1,0:T(4,128)(2,1)} fusion(bf16[64,3,64]{2,1,0:T(4,128)(2,1)S(1)} %copy.107, s32[1024]{0:T(1024)S(1)} %pad_clamp_fusion), kind=kCustom, calls=%fused_computation.1 | custom fusion | bytes 247040 | tf_op jit(solution)/shard_map/jit(_take)/gather | solution.py:47
  85.5 39.8 %select_select_fusion = s32[320]{0:T(512)S(1)} fusion(s32[]{:T(128)} %bitcast.5, s32[]{:T(128)} %bitcast.6, s32[]{:T(128)} %bitcast.7, s32[]{:T(128)} %bitcast.8, s32[]{:T(128)} %bitcast.9, s32[]{:T(128)} %bitcast.10, s32[]{:T(128)} %bitcast.11, s32[]{:T(128)} %bitcast.12, s32[]{:T(128)} %bitcast.13, s32[]{:T(128)} %bitcast.14, s32[]{:T(128)} %bitcast.15, ...), kind=kLoop, calls=%fused_computation.96 | loop fusion | flops 42880 | bytes 2816 | tf_op jit(solution)/shard_map/jit(_take)/select_n | solution.py:45
  125.4 0.9 fusion.36
  126.3 5.7 %fusion.70 = (f32[320,3]{1,0:T(8,128)}, f32[320,3,128]{2,1,0:T(4,128)}) fusion(bf16[320,1,128,128]{3,2,0,1:T(8,128)(2,1)} %bitcast.182, bf16[320,3,64]{2,1,0:T(4,128)(2,1)} %gather_fusion.1, pred[320]{0:T(512)(128)(4,1)} %get-tuple-element.16, pred[320,128]{1,0:T(8,128)(4,1)S(1)} %fusion.36), kind=kOutput, calls=%fused_computation.124 | convolution fusion | flops 16157760 | bytes 6107392 | tf_op jit(solution)/shard_map/pkgd,pkdt->pkgt/dot_general | solution.py:49
  131.9 1.0 copy.109
  132.9 0.9 fusion.48
  134.2 1.6 gather_fusion.2
  135.8 1.0 broadcast_select_fusion
  136.9 1.9 fusion.19
  138.8 6.5 %fusion.2 = f32[320,3,64]{2,1,0:T(4,128)} fusion(bf16[320,1,128,128]{3,2,0,1:T(8,128)(2,1)} %bitcast.183, f32[320,3,128]{2,1,0:T(4,128)} %get-tuple-element.82, f32[320,3]{1,0:T(8,128)S(1)} %broadcast_select_fusion, pred[320,128]{1,0:T(8,128)(4,1)S(1)} %fusion.36), kind=kOutput, calls=%fused_computation.9 | convolution fusion | flops 16097280 | bytes 6188800 | tf_op jit(solution)/shard_map/pkgt,pkdt->pkgd/dot_general | solution.py:72
  145.5 2.1 copy.112
  147.5 2.0 fusion.15
  149.5 0.9 copy.113
  150.4 2.0 convolution_convert_fusion
  153.3 28.5 %reduce-scatter.2.cloned.1.call-done = bf16[8,1536]{1,0:T(8,128)(2,1)} async-done(((bf16[64,1536]{1,0:T(8,128)(2,1)}), bf16[8,1536]{1,0:T(8,128)(2,1)}) %reduce-scatter.2.cloned.1.call-update) | async-done | bytes 24592 | tf_op jit(solution)/shard_map/reduce_scatter | solution.py:132
  181.9 0.9 fusion.41
  184.7 6.8 %all-to-all-start = ((bf16[16,2,1,1536]{3,1,2,0:T(2,128)(2,1)}), bf16[16,2,1,1536]{3,1,2,0:T(2,128)(2,1)S(1)}, u32[]{:S(2)}, u32[]{:S(2)}) async-start(bf16[16,2,1,1536]{3,1,2,0:T(2,128)(2,1)} %bitcast.90), calls=%async_computation.1 | async-start | bytes 196608 | tf_op jit(solution)/shard_map/all_to_all | solution.py:168
  191.7 7.7 %all-to-all-done = bf16[16,2,1,1536]{3,1,2,0:T(2,128)(2,1)S(1)} async-done(((bf16[16,2,1,1536]{3,1,2,0:T(2,128)(2,1)}), bf16[16,2,1,1536]{3,1,2,0:T(2,128)(2,1)S(1)}, u32[]{:S(2)}, u32[]{:S(2)}) %all-to-all-start) | async-done | bytes 98336 | tf_op jit(solution)/shard_map/all_to_all | solution.py:168
  199.4 4.0 %fusion.6 = f32[1,32,2048]{2,1,0:T(8,128)S(1)} fusion(bf16[32,1536]{1,0:T(8,128)(2,1)S(1)} %reshape.352, bf16[1,1536,2048]{2,1,0:T(8,128)(2,1)} %param.24), kind=kOutput, calls=%fused_computation.15 | convolution fusion | flops 201326592 | bytes 6651904 | tf_op jit(solution)/shard_map/erd,edf->erf/dot_general | solution.py:95
  204.6 3.5 %all-to-all-start.1 = ((bf16[16,2,1,1536]{3,1,2,0:T(2,128)(2,1)}), bf16[16,2,1,1536]{3,1,2,0:T(2,128)(2,1)S(1)}, u32[]{:S(2)}, u32[]{:S(2)}) async-start(bf16[16,2,1,1536]{3,1,2,0:T(2,128)(2,1)} %bitcast.95), calls=%async_computation.2 | async-start | bytes 196608 | tf_op jit(solution)/shard_map/all_to_all | solution.py:169
  208.3 7.6 %all-to-all-done.1 = bf16[16,2,1,1536]{3,1,2,0:T(2,128)(2,1)S(1)} async-done(((bf16[16,2,1,1536]{3,1,2,0:T(2,128)(2,1)}), bf16[16,2,1,1536]{3,1,2,0:T(2,128)(2,1)S(1)}, u32[]{:S(2)}, u32[]{:S(2)}) %all-to-all-start.1) | async-done | bytes 98336 | tf_op jit(solution)/shard_map/all_to_all | solution.py:169
  (71 shorter events, 12.8 us)
Async XLA Ops:
  6.5 196.8 %copy-start = (bf16[1,1024,1536]{2,1,0:T(8,128)(2,1)S(1)}, bf16[1,1024,1536]{2,1,0:T(8,128)(2,1)}, u32[]{:S(2)}) copy-start(bf16[1,1024,1536]{2,1,0:T(8,128)(2,1)} %param.25) | copy-start | bytes 9437188
  6.5 175.3 %reduce-scatter.2.cloned.1.call-start = ((), (), s32[]{:S(2)}) async-start(), calls=%async_computation.3 | async-start | bytes 221184 | tf_op jit(solution)/shard_map/reduce_scatter | solution.py:132
  134.2 18.2 %copy-start.3 = (s32[8,2]{0,1:T(2,128)S(1)}, s32[8,2]{0,1:T(2,128)}, u32[]{:S(2)}) copy-start(s32[8,2]{0,1:T(2,128)} %param.23) | copy-start | bytes 196
  134.2 48.5 %copy-start.2 = (f32[1536]{0:T(1024)S(1)}, f32[1536]{0:T(1024)}, u32[]{:S(2)}) copy-start(f32[1536]{0:T(1024)} %param.21) | copy-start | bytes 18436
  134.2 48.6 %copy-start.1 = (bf16[1536,16]{0,1:T(8,128)(2,1)S(1)}, bf16[1536,16]{0,1:T(8,128)(2,1)}, u32[]{:S(2)}) copy-start(bf16[1536,16]{0,1:T(8,128)(2,1)} %param.22) | copy-start | bytes 147460
  184.7 14.6 %all-to-all-start = ((bf16[16,2,1,1536]{3,1,2,0:T(2,128)(2,1)}), bf16[16,2,1,1536]{3,1,2,0:T(2,128)(2,1)S(1)}, u32[]{:S(2)}, u32[]{:S(2)}) async-start(bf16[16,2,1,1536]{3,1,2,0:T(2,128)(2,1)} %bitcast.90), calls=%async_computation.1 | async-start | bytes 196608 | tf_op jit(solution)/shard_map/all_to_all | solution.py:168
  204.6 11.3 %all-to-all-start.1 = ((bf16[16,2,1,1536]{3,1,2,0:T(2,128)(2,1)}), bf16[16,2,1,1536]{3,1,2,0:T(2,128)(2,1)S(1)}, u32[]{:S(2)}, u32[]{:S(2)}) async-start(bf16[16,2,1,1536]{3,1,2,0:T(2,128)(2,1)} %bitcast.95), calls=%async_computation.2 | async-start | bytes 196608 | tf_op jit(solution)/shard_map/all_to_all | solution.py:169
Sparse Core Ops, SparseCore 0:
  152.5 29.2 reduce-scatter.1
where the time goes:
time: 225 us; the launch traced here: 224 us
  other arithmetic  51.4 us (23%)
  waiting for transfers between devices  43.9 us (20%)
  blocking collectives  40.8 us (18%)
  local copies, waits for them, and re-layouts  39.5 us (18%)
  matrix products  24.1 us (11%)
  between operations  13.6 us (6%)
  starting transfers between devices  10.3 us (5%)
    select_n x2, other arithmetic, attend(): jnp.take(seq_lens, owner_safe)[:, None]  40.4 us
    reduce_scatter x1, waiting for transfers between devices, shards(): lax.psum_scatter(jnp.dot(head_out, out_flat, preferred_element_type=jnp.f...  28.5 us
    all_gather x1, blocking collectives, shards(): every_row = lax.all_gather(hidden, 'req', axis=0, tiled=True)  26.8 us
    all_gather x1, blocking collectives, shards(): tokens = lax.all_gather(picked_rows, 'kv', axis=1, tiled=True)  14 us
    scatter x1, local copies, waits for them, and re-layouts, attend(): jnp.zeros((pool_pages,), jnp.int32).at[target_page]  8.21 us
    scatter x1, local copies, waits for them, and re-layouts, attend(): jnp.full((pool_pages,), slot_count, jnp.int32).at[target_page]  8.03 us
    gather x4, local copies, waits for them, and re-layouts, attend(): jnp.take(seq_lens, owner_safe)[:, None]  7.79 us
    all_to_all x1, waiting for transfers between devices, shards(): lax.all_to_all(outgoing, 'req', split_axis=0, concat_axis=0, tiled=True)  7.69 us
  transfers between devices with their start and end apart: 3, of which 3 were waited for; matrix products, arithmetic and copies ran while one was open for 1% of the time, Pallas kernels for 0%

commit v1 on v0

--- a/solution.py
+++ b/solution.py
@@ -166,9 +166,20 @@
     )
     outgoing = outgoing.astype(jnp.bfloat16).reshape(n_req, capacity, local_experts, width)
     arrived = lax.all_to_all(outgoing, "req", split_axis=0, concat_axis=0, tiled=True)
-    returned = lax.all_to_all(
-        expert_apply(arrived, gate_up, down), "req", split_axis=0, concat_axis=0, tiled=True
-    )
+    x = expert_apply(arrived, gate_up, down)
+    ways, here = (lax.axis_size("req"), lax.axis_index("req"))
+    width_2 = x.shape[0] // ways
+    lengths = list(x.shape)
+    lengths[0] = width_2
+    height = lengths[0]
+    lengths[0] = height * ways
+    full = jnp.zeros(lengths, x.dtype)
+    for mask in range(ways):
+        part = lax.dynamic_slice_in_dim(x, (here ^ mask) * width_2, width_2, axis=0)
+        if mask:
+            part = lax.ppermute(part, "req", [(d, d ^ mask) for d in range(ways)])
+        full = lax.dynamic_update_slice_in_dim(full, part, (here ^ mask) * height, axis=0)
+    returned = full
     back_rows = returned.reshape(experts_all * capacity, width)
     paired_output = jnp.dot(placement_plan, back_rows, preferred_element_type=jnp.float32).reshape(
         sub_rows, 2, width

time: 225 us -> 244 us (1.084)
  starting transfers between devices: 10.3 us -> 38.9 us
  waiting for transfers between devices: 43.9 us -> 38.6 us
  other arithmetic: 51.4 us -> 48.6 us
    ppermute x0 -> x15, starting transfers between devices: none -> 32.1 us  [shards(): part = lax.ppermute(part, 'req', [(d, d ^ mask) for d in range(ways)])]
    all_to_all x1 -> x0, waiting for transfers between devices: 7.62 us -> none  [shards(): lax.all_to_all(expert_apply(arrived, gate_up, down), 'req', split_axis=0,...]
    all_to_all x1 -> x0, starting transfers between devices: 3.51 us -> none  [shards(): lax.all_to_all(expert_apply(arrived, gate_up, down), 'req', split_axis=0,...]
    ppermute x0 -> x15, waiting for transfers between devices: none -> 3.17 us  [shards(): part = lax.ppermute(part, 'req', [(d, d ^ mask) for d in range(ways)])]
  transfers between devices with their start and end apart: 3 -> 17, of which waited for: 3 -> 3; matrix products, arithmetic and copies ran while one was open for 1% -> 1% of each run, Pallas kernels for 0% -> 0%
where the time goes in v1:
time: 244 us; the launch traced here: 243 us
  other arithmetic  48.6 us (20%)
  blocking collectives  40.8 us (17%)
  local copies, waits for them, and re-layouts  39.2 us (16%)
  starting transfers between devices  38.9 us (16%)
  waiting for transfers between devices  38.6 us (16%)
  matrix products  22.8 us (9%)
  between operations  13.9 us (6%)
    select_n x2, other arithmetic, attend(): jnp.take(seq_lens, owner_safe)[:, None]  40 us
    ppermute x15, starting transfers between devices, shards(): part = lax.ppermute(part, 'req', [(d, d ^ mask) for d in range(ways)])  32.1 us
    reduce_scatter x1, waiting for transfers between devices, shards(): lax.psum_scatter(jnp.dot(head_out, out_flat, preferred_element_type=jnp.f...  27.8 us
    all_gather x1, blocking collectives, shards(): every_row = lax.all_gather(hidden, 'req', axis=0, tiled=True)  26.8 us
    all_gather x1, blocking collectives, shards(): tokens = lax.all_gather(picked_rows, 'kv', axis=1, tiled=True)  14 us
    scatter x1, local copies, waits for them, and re-layouts, attend(): jnp.zeros((pool_pages,), jnp.int32).at[target_page]  8.21 us
    scatter x1, local copies, waits for them, and re-layouts, attend(): jnp.full((pool_pages,), slot_count, jnp.int32).at[target_page]  8.03 us
    gather x4, local copies, waits for them, and re-layouts, attend(): jnp.take(seq_lens, owner_safe)[:, None]  7.78 us
  transfers between devices with their start and end apart: 17, of which 3 were waited for; matrix products, arithmetic and copies ran while one was open for 1% of the time, Pallas kernels for 0%

profile of v1, /device:TPU:0, one launch (start us, length us, event | category | flops | bytes accessed | tf_op | source)
XLA Modules:
  0.0 243.0 jit_solution(4763796137871690094)
XLA Ops:
  6.5 2.1 fusion.66
  8.6 2.1 fusion.67
  10.7 2.1 fusion.68
  13.4 1.6 fusion.69
  16.0 8.0 %scatter_custom_fusion = s32[320]{0:T(512)S(1)} fusion(s32[2048]{0:T(1024)S(1)} %bitcast.179, s32[2048]{0:T(1024)S(1)} %reshape.468, s32[]{:T(128)} %constant.87.clone.1), kind=kCustom, calls=%fused_computation.144 | custom fusion | bytes 1284 | tf_op jit(solution)/shard_map/scatter | solution.py:40
  24.9 26.8 %all_gather.6 = bf16[1024,192]{1,0:T(8,128)(2,1)} all-gather(bf16[64,192]{1,0:T(8,128)(2,1)} %param.13), channel_id=1, replica_groups=mesh['req'=16,'kv'=8] {'req'}, dimensions={0}, use_global_device_ids=true | all-gather | bytes 417792 | tf_op jit(solution)/shard_map/all_gather | solution.py:123
  51.7 1.8 gather_fusion
  53.5 14.0 %all-gather = bf16[8,192,64]{1,2,0:T(8,128)(2,1)S(1)} all-gather(bf16[1,192,64]{1,2,0:T(8,128)(2,1)S(1)} %select_bitcast_fusion), channel_id=1, replica_groups=mesh['req'=16,'kv'=8] {'kv'}, dimensions={0}, use_global_device_ids=true | all-gather | bytes 221184 | tf_op jit(solution)/shard_map/all_gather | solution.py:126
  68.4 1.2 reshape.494
  69.8 1.7 convolution_bitcast_fusion
  72.1 8.2 %scatter_custom_fusion.1 = s32[320]{0:T(512)S(1)} fusion(s32[2048]{0:T(1024)S(1)} %bitcast.180, s32[2048]{0:T(1024)S(1)} %reshape.476, s32[]{:T(128)} %constant.88.clone.1), kind=kCustom, calls=%fused_computation.141 | custom fusion | bytes 1284 | tf_op jit(solution)/shard_map/scatter | solution.py:42
  80.6 2.5 %gather_fusion.1 = bf16[320,3,64]{2,1,0:T(4,128)(2,1)} fusion(bf16[64,3,64]{2,1,0:T(4,128)(2,1)S(1)} %copy.105, s32[1024]{0:T(1024)S(1)} %pad_clamp_fusion), kind=kCustom, calls=%fused_computation.1 | custom fusion | bytes 247040 | tf_op jit(solution)/shard_map/jit(_take)/gather | solution.py:47
  83.1 40.0 %select_select_fusion = s32[320]{0:T(512)S(1)} fusion(s32[]{:T(128)} %bitcast.5, s32[]{:T(128)} %bitcast.6, s32[]{:T(128)} %bitcast.7, s32[]{:T(128)} %bitcast.8, s32[]{:T(128)} %bitcast.9, s32[]{:T(128)} %bitcast.10, s32[]{:T(128)} %bitcast.11, s32[]{:T(128)} %bitcast.12, s32[]{:T(128)} %bitcast.13, s32[]{:T(128)} %bitcast.14, s32[]{:T(128)} %bitcast.15, ...), kind=kLoop, calls=%fused_computation.128 | loop fusion | flops 42880 | bytes 2816 | tf_op jit(solution)/shard_map/jit(_take)/select_n | solution.py:45
  123.9 5.7 %fusion.70 = (f32[320,3]{1,0:T(8,128)}, f32[320,3,128]{2,1,0:T(4,128)}) fusion(bf16[320,1,128,128]{3,2,0,1:T(8,128)(2,1)} %bitcast.181, bf16[320,3,64]{2,1,0:T(4,128)(2,1)} %gather_fusion.1, pred[320]{0:T(512)(128)(4,1)S(1)} %get-tuple-element.32, pred[320,128]{1,0:T(8,128)(4,1)S(1)} %fusion.36), kind=kOutput, calls=%fused_computation.156 | convolution fusion | flops 16157760 | bytes 6107200 | tf_op jit(solution)/shard_map/pkgd,pkdt->pkgt/dot_general | solution.py:49
  133.5 1.9 fusion.19
  135.4 6.5 %fusion.2 = f32[320,3,64]{2,1,0:T(4,128)} fusion(bf16[320,1,128,128]{3,2,0,1:T(8,128)(2,1)} %bitcast.182, f32[320,3,128]{2,1,0:T(4,128)} %get-tuple-element.98, f32[320,3]{1,0:T(8,128)S(1)} %broadcast_select_fusion, pred[320,128]{1,0:T(8,128)(4,1)} %copy-done.1), kind=kOutput, calls=%fused_computation.9 | convolution fusion | flops 16097280 | bytes 6188800 | tf_op jit(solution)/shard_map/pkgt,pkdt->pkgd/dot_general | solution.py:72
  142.1 2.1 copy.110
  144.2 1.3 fusion.15
  145.7 2.0 convolution_convert_fusion
  149.4 27.8 %reduce-scatter.2.cloned.1.call-done = bf16[8,1536]{1,0:T(8,128)(2,1)} async-done(((bf16[64,1536]{1,0:T(8,128)(2,1)}), bf16[8,1536]{1,0:T(8,128)(2,1)}) %reduce-scatter.2.cloned.1.call-update) | async-done | bytes 24592 | tf_op jit(solution)/shard_map/reduce_scatter | solution.py:132
  180.0 6.8 %all-to-all-start = ((bf16[16,2,1,1536]{3,1,2,0:T(2,128)(2,1)}), bf16[16,2,1,1536]{3,1,2,0:T(2,128)(2,1)S(1)}, u32[]{:S(2)}, u32[]{:S(2)}) async-start(bf16[16,2,1,1536]{3,1,2,0:T(2,128)(2,1)} %bitcast.90), calls=%async_computation.1 | async-start | bytes 196608 | tf_op jit(solution)/shard_map/all_to_all | solution.py:168
  186.9 7.7 %all-to-all-done = bf16[16,2,1,1536]{3,1,2,0:T(2,128)(2,1)S(1)} async-done(((bf16[16,2,1,1536]{3,1,2,0:T(2,128)(2,1)}), bf16[16,2,1,1536]{3,1,2,0:T(2,128)(2,1)S(1)}, u32[]{:S(2)}, u32[]{:S(2)}) %all-to-all-start) | async-done | bytes 98336 | tf_op jit(solution)/shard_map/all_to_all | solution.py:168
  194.6 4.0 %fusion.6 = f32[1,32,2048]{2,1,0:T(8,128)S(1)} fusion(bf16[32,1536]{1,0:T(8,128)(2,1)S(1)} %reshape.352, bf16[1,1536,2048]{2,1,0:T(8,128)(2,1)} %param.24), kind=kOutput, calls=%fused_computation.15 | convolution fusion | flops 201326592 | bytes 6651904 | tf_op jit(solution)/shard_map/erd,edf->erf/dot_general | solution.py:95
  200.3 2.0 collective-permute-start.1
  202.3 2.2 collective-permute-start.2
  205.3 3.2 %collective-permute-start.5 = (bf16[1,2,1,1536]{3,1,0,2:T(2,128)(2,1)S(1)}, bf16[1,2,1,1536]{3,1,0,2:T(2,128)(2,1)S(1)}, u32[]{:S(2)}, u32[]{:S(2)}) collective-permute-start(bf16[1,2,1,1536]{3,1,0,2:T(2,128)(2,1)S(1)} %get-tuple-element.18), channel_id=1, source_target_pairs={{0,48},{8,56},{16,32},{24,40},{32,16},{40,24},{48,0},{56,8},{64,11... | collective-permute-start | bytes 18440 | tf_op jit(solution)/shard_map/ppermute | solution.py:180
  208.5 3.1 %collective-permute-start.6 = (bf16[1,2,1,1536]{3,1,0,2:T(2,128)(2,1)S(1)}, bf16[1,2,1,1536]{3,1,0,2:T(2,128)(2,1)S(1)}, u32[]{:S(2)}, u32[]{:S(2)}) collective-permute-start(bf16[1,2,1,1536]{3,1,0,2:T(2,128)(2,1)S(1)} %get-tuple-element.17), channel_id=1, source_target_pairs={{0,56},{8,48},{16,40},{24,32},{32,24},{40,16},{48,8},{56,0},{64,12... | collective-permute-start | bytes 18440 | tf_op jit(solution)/shard_map/ppermute | solution.py:180
  213.0 5.1 %collective-permute-start.9 = (bf16[1,2,1,1536]{3,1,0,2:T(2,128)(2,1)S(1)}, bf16[1,2,1,1536]{3,1,0,2:T(2,128)(2,1)S(1)}, u32[]{:S(2)}, u32[]{:S(2)}) collective-permute-start(bf16[1,2,1,1536]{3,1,0,2:T(2,128)(2,1)S(1)} %get-tuple-element.14), channel_id=1, source_target_pairs={{0,80},{8,88},{16,64},{24,72},{32,112},{40,120},{48,96},{56,104},{... | collective-permute-start | bytes 18440 | tf_op jit(solution)/shard_map/ppermute | solution.py:180
  218.1 4.0 %collective-permute-start.10 = (bf16[1,2,1,1536]{3,1,0,2:T(2,128)(2,1)S(1)}, bf16[1,2,1,1536]{3,1,0,2:T(2,128)(2,1)S(1)}, u32[]{:S(2)}, u32[]{:S(2)}) collective-permute-start(bf16[1,2,1,1536]{3,1,0,2:T(2,128)(2,1)S(1)} %get-tuple-element.13), channel_id=1, source_target_pairs={{0,88},{8,80},{16,72},{24,64},{32,120},{40,112},{48,104},{56,96},{... | collective-permute-start | bytes 18440 | tf_op jit(solution)/shard_map/ppermute | solution.py:180
  223.3 4.9 %collective-permute-start.13 = (bf16[1,2,1,1536]{3,1,0,2:T(2,128)(2,1)S(1)}, bf16[1,2,1,1536]{3,1,0,2:T(2,128)(2,1)S(1)}, u32[]{:S(2)}, u32[]{:S(2)}) collective-permute-start(bf16[1,2,1,1536]{3,1,0,2:T(2,128)(2,1)S(1)} %get-tuple-element.10), channel_id=1, source_target_pairs={{0,112},{8,120},{16,96},{24,104},{32,80},{40,88},{48,64},{56,72},{... | collective-permute-start | bytes 18440 | tf_op jit(solution)/shard_map/ppermute | solution.py:180
  228.2 3.8 %collective-permute-start.14 = (bf16[1,2,1,1536]{3,1,0,2:T(2,128)(2,1)S(1)}, bf16[1,2,1,1536]{3,1,0,2:T(2,128)(2,1)S(1)}, u32[]{:S(2)}, u32[]{:S(2)}) collective-permute-start(bf16[1,2,1,1536]{3,1,0,2:T(2,128)(2,1)S(1)} %get-tuple-element.9), channel_id=1, source_target_pairs={{0,120},{8,112},{16,104},{24,96},{32,88},{40,80},{48,72},{56,64},{... | collective-permute-start | bytes 18440 | tf_op jit(solution)/shard_map/ppermute | solution.py:180
  232.1 3.1 %collective-permute-done.14 = bf16[1,2,1,1536]{3,1,0,2:T(2,128)(2,1)S(1)} collective-permute-done((bf16[1,2,1,1536]{3,1,0,2:T(2,128)(2,1)S(1)}, bf16[1,2,1,1536]{3,1,0,2:T(2,128)(2,1)S(1)}, u32[]{:S(2)}, u32[]{:S(2)}) %collective-permute-start.14) | collective-permute-done | bytes 6176 | tf_op jit(solution)/shard_map/ppermute | solution.py:180
  (122 shorter events, 20.1 us)
Async XLA Ops:
  6.5 192.1 %copy-start = (bf16[1,1024,1536]{2,1,0:T(8,128)(2,1)S(1)}, bf16[1,1024,1536]{2,1,0:T(8,128)(2,1)}, u32[]{:S(2)}) copy-start(bf16[1,1024,1536]{2,1,0:T(8,128)(2,1)} %param.25) | copy-start | bytes 9437188
  6.5 170.6 %reduce-scatter.2.cloned.1.call-start = ((), (), s32[]{:S(2)}) async-start(), calls=%async_computation.2 | async-start | bytes 221184 | tf_op jit(solution)/shard_map/reduce_scatter | solution.py:132
  24.1 106.5 %copy-start.6 = (pred[320]{0:T(512)(128)(4,1)}, pred[320]{0:T(512)(128)(4,1)S(1)}, u32[]{:S(2)}) copy-start(pred[320]{0:T(512)(128)(4,1)S(1)} %get-tuple-element.32) | copy-start | bytes 964
  123.2 0.6 copy-start.1
  132.7 11.5 %copy-start.5 = (bf16[64,1,3]{0,2,1:T(4,128)(2,1)S(1)}, bf16[64,1,3]{0,2,1:T(4,128)(2,1)}, u32[]{:S(2)}) copy-start(bf16[64,1,3]{0,2,1:T(4,128)(2,1)} %get-tuple-element.29) | copy-start | bytes 1156
  132.7 11.5 %copy-start.3 = (f32[64,64]{1,0:T(8,128)S(1)}, f32[64,64]{1,0:T(8,128)}, u32[]{:S(2)}) copy-start(f32[64,64]{1,0:T(8,128)} %get-tuple-element.25) | copy-start | bytes 49156
  133.5 44.5 %copy-start.4 = (f32[1536]{0:T(1024)S(1)}, f32[1536]{0:T(1024)}, u32[]{:S(2)}) copy-start(f32[1536]{0:T(1024)} %param.21) | copy-start | bytes 18436
  133.5 44.6 %copy-start.2 = (bf16[1536,16]{0,1:T(8,128)(2,1)S(1)}, bf16[1536,16]{0,1:T(8,128)(2,1)}, u32[]{:S(2)}) copy-start(bf16[1536,16]{0,1:T(8,128)(2,1)} %param.22) | copy-start | bytes 147460
  180.0 14.6 %all-to-all-start = ((bf16[16,2,1,1536]{3,1,2,0:T(2,128)(2,1)}), bf16[16,2,1,1536]{3,1,2,0:T(2,128)(2,1)S(1)}, u32[]{:S(2)}, u32[]{:S(2)}) async-start(bf16[16,2,1,1536]{3,1,2,0:T(2,128)(2,1)} %bitcast.90), calls=%async_computation.1 | async-start | bytes 196608 | tf_op jit(solution)/shard_map/all_to_all | solution.py:168
  199.5 5.8 %collective-permute-start = (bf16[1,2,1,1536]{3,1,0,2:T(2,128)(2,1)S(1)}, bf16[1,2,1,1536]{3,1,0,2:T(2,128)(2,1)S(1)}, u32[]{:S(2)}, u32[]{:S(2)}) collective-permute-start(bf16[1,2,1,1536]{3,1,0,2:T(2,128)(2,1)S(1)} %get-tuple-element.23), channel_id=1, source_target_pairs={{0,8},{8,0},{16,24},{24,16},{32,40},{40,32},{48,56},{56,48},{64,72... | collective-permute-start | bytes 18440 | tf_op jit(solution)/shard_map/ppermute | solution.py:180
  200.3 8.2 %collective-permute-start.1 = (bf16[1,2,1,1536]{3,1,0,2:T(2,128)(2,1)S(1)}, bf16[1,2,1,1536]{3,1,0,2:T(2,128)(2,1)S(1)}, u32[]{:S(2)}, u32[]{:S(2)}) collective-permute-start(bf16[1,2,1,1536]{3,1,0,2:T(2,128)(2,1)S(1)} %get-tuple-element.22), channel_id=1, source_target_pairs={{0,16},{8,24},{16,0},{24,8},{32,48},{40,56},{48,32},{56,40},{64,80... | collective-permute-start | bytes 18440 | tf_op jit(solution)/shard_map/ppermute | solution.py:180
  202.3 9.4 %collective-permute-start.2 = (bf16[1,2,1,1536]{3,1,0,2:T(2,128)(2,1)S(1)}, bf16[1,2,1,1536]{3,1,0,2:T(2,128)(2,1)S(1)}, u32[]{:S(2)}, u32[]{:S(2)}) collective-permute-start(bf16[1,2,1,1536]{3,1,0,2:T(2,128)(2,1)S(1)} %get-tuple-element.21), channel_id=1, source_target_pairs={{0,24},{8,16},{16,8},{24,0},{32,56},{40,48},{48,40},{56,32},{64,88... | collective-permute-start | bytes 18440 | tf_op jit(solution)/shard_map/ppermute | solution.py:180
  204.4 8.4 %collective-permute-start.3 = (bf16[1,2,1,1536]{3,1,0,2:T(2,128)(2,1)S(1)}, bf16[1,2,1,1536]{3,1,0,2:T(2,128)(2,1)S(1)}, u32[]{:S(2)}, u32[]{:S(2)}) collective-permute-start(bf16[1,2,1,1536]{3,1,0,2:T(2,128)(2,1)S(1)} %get-tuple-element.20), channel_id=1, source_target_pairs={{0,32},{8,40},{16,48},{24,56},{32,0},{40,8},{48,16},{56,24},{64,96... | collective-permute-start | bytes 18440 | tf_op jit(solution)/shard_map/ppermute | solution.py:180
  204.8 8.1 %collective-permute-start.4 = (bf16[1,2,1,1536]{3,1,0,2:T(2,128)(2,1)S(1)}, bf16[1,2,1,1536]{3,1,0,2:T(2,128)(2,1)S(1)}, u32[]{:S(2)}, u32[]{:S(2)}) collective-permute-start(bf16[1,2,1,1536]{3,1,0,2:T(2,128)(2,1)S(1)} %get-tuple-element.19), channel_id=1, source_target_pairs={{0,40},{8,32},{16,56},{24,48},{32,8},{40,0},{48,24},{56,16},{64,10... | collective-permute-start | bytes 18440 | tf_op jit(solution)/shard_map/ppermute | solution.py:180
  205.3 12.8 %collective-permute-start.5 = (bf16[1,2,1,1536]{3,1,0,2:T(2,128)(2,1)S(1)}, bf16[1,2,1,1536]{3,1,0,2:T(2,128)(2,1)S(1)}, u32[]{:S(2)}, u32[]{:S(2)}) collective-permute-start(bf16[1,2,1,1536]{3,1,0,2:T(2,128)(2,1)S(1)} %get-tuple-element.18), channel_id=1, source_target_pairs={{0,48},{8,56},{16,32},{24,40},{32,16},{40,24},{48,0},{56,8},{64,11... | collective-permute-start | bytes 18440 | tf_op jit(solution)/shard_map/ppermute | solution.py:180
  208.5 13.6 %collective-permute-start.6 = (bf16[1,2,1,1536]{3,1,0,2:T(2,128)(2,1)S(1)}, bf16[1,2,1,1536]{3,1,0,2:T(2,128)(2,1)S(1)}, u32[]{:S(2)}, u32[]{:S(2)}) collective-permute-start(bf16[1,2,1,1536]{3,1,0,2:T(2,128)(2,1)S(1)} %get-tuple-element.17), channel_id=1, source_target_pairs={{0,56},{8,48},{16,40},{24,32},{32,24},{40,16},{48,8},{56,0},{64,12... | collective-permute-start | bytes 18440 | tf_op jit(solution)/shard_map/ppermute | solution.py:180
  211.6 11.6 %collective-permute-start.7 = (bf16[1,2,1,1536]{3,1,0,2:T(2,128)(2,1)S(1)}, bf16[1,2,1,1536]{3,1,0,2:T(2,128)(2,1)S(1)}, u32[]{:S(2)}, u32[]{:S(2)}) collective-permute-start(bf16[1,2,1,1536]{3,1,0,2:T(2,128)(2,1)S(1)} %get-tuple-element.16), channel_id=1, source_target_pairs={{0,64},{8,72},{16,80},{24,88},{32,96},{40,104},{48,112},{56,120},{... | collective-permute-start | bytes 18440 | tf_op jit(solution)/shard_map/ppermute | solution.py:180
  212.8 10.5 %collective-permute-start.8 = (bf16[1,2,1,1536]{3,1,0,2:T(2,128)(2,1)S(1)}, bf16[1,2,1,1536]{3,1,0,2:T(2,128)(2,1)S(1)}, u32[]{:S(2)}, u32[]{:S(2)}) collective-permute-start(bf16[1,2,1,1536]{3,1,0,2:T(2,128)(2,1)S(1)} %get-tuple-element.15), channel_id=1, source_target_pairs={{0,72},{8,64},{16,88},{24,80},{32,104},{40,96},{48,120},{56,112},{... | collective-permute-start | bytes 18440 | tf_op jit(solution)/shard_map/ppermute | solution.py:180
  213.0 15.3 %collective-permute-start.9 = (bf16[1,2,1,1536]{3,1,0,2:T(2,128)(2,1)S(1)}, bf16[1,2,1,1536]{3,1,0,2:T(2,128)(2,1)S(1)}, u32[]{:S(2)}, u32[]{:S(2)}) collective-permute-start(bf16[1,2,1,1536]{3,1,0,2:T(2,128)(2,1)S(1)} %get-tuple-element.14), channel_id=1, source_target_pairs={{0,80},{8,88},{16,64},{24,72},{32,112},{40,120},{48,96},{56,104},{... | collective-permute-start | bytes 18440 | tf_op jit(solution)/shard_map/ppermute | solution.py:180
  218.1 13.9 %collective-permute-start.10 = (bf16[1,2,1,1536]{3,1,0,2:T(2,128)(2,1)S(1)}, bf16[1,2,1,1536]{3,1,0,2:T(2,128)(2,1)S(1)}, u32[]{:S(2)}, u32[]{:S(2)}) collective-permute-start(bf16[1,2,1,1536]{3,1,0,2:T(2,128)(2,1)S(1)} %get-tuple-element.13), channel_id=1, source_target_pairs={{0,88},{8,80},{16,72},{24,64},{32,120},{40,112},{48,104},{56,96},{... | collective-permute-start | bytes 18440 | tf_op jit(solution)/shard_map/ppermute | solution.py:180
  222.1 9.9 %collective-permute-start.11 = (bf16[1,2,1,1536]{3,1,0,2:T(2,128)(2,1)S(1)}, bf16[1,2,1,1536]{3,1,0,2:T(2,128)(2,1)S(1)}, u32[]{:S(2)}, u32[]{:S(2)}) collective-permute-start(bf16[1,2,1,1536]{3,1,0,2:T(2,128)(2,1)S(1)} %get-tuple-element.12), channel_id=1, source_target_pairs={{0,96},{8,104},{16,112},{24,120},{32,64},{40,72},{48,80},{56,88},{... | collective-permute-start | bytes 18440 | tf_op jit(solution)/shard_map/ppermute | solution.py:180
  223.2 8.8 %collective-permute-start.12 = (bf16[1,2,1,1536]{3,1,0,2:T(2,128)(2,1)S(1)}, bf16[1,2,1,1536]{3,1,0,2:T(2,128)(2,1)S(1)}, u32[]{:S(2)}, u32[]{:S(2)}) collective-permute-start(bf16[1,2,1,1536]{3,1,0,2:T(2,128)(2,1)S(1)} %get-tuple-element.11), channel_id=1, source_target_pairs={{0,104},{8,96},{16,120},{24,112},{32,72},{40,64},{48,88},{56,80},{... | collective-permute-start | bytes 18440 | tf_op jit(solution)/shard_map/ppermute | solution.py:180
  223.3 8.8 %collective-permute-start.13 = (bf16[1,2,1,1536]{3,1,0,2:T(2,128)(2,1)S(1)}, bf16[1,2,1,1536]{3,1,0,2:T(2,128)(2,1)S(1)}, u32[]{:S(2)}, u32[]{:S(2)}) collective-permute-start(bf16[1,2,1,1536]{3,1,0,2:T(2,128)(2,1)S(1)} %get-tuple-element.10), channel_id=1, source_target_pairs={{0,112},{8,120},{16,96},{24,104},{32,80},{40,88},{48,64},{56,72},{... | collective-permute-start | bytes 18440 | tf_op jit(solution)/shard_map/ppermute | solution.py:180
  228.2 7.0 %collective-permute-start.14 = (bf16[1,2,1,1536]{3,1,0,2:T(2,128)(2,1)S(1)}, bf16[1,2,1,1536]{3,1,0,2:T(2,128)(2,1)S(1)}, u32[]{:S(2)}, u32[]{:S(2)}) collective-permute-start(bf16[1,2,1,1536]{3,1,0,2:T(2,128)(2,1)S(1)} %get-tuple-element.9), channel_id=1, source_target_pairs={{0,120},{8,112},{16,104},{24,96},{32,88},{40,80},{48,72},{56,64},{... | collective-permute-start | bytes 18440 | tf_op jit(solution)/shard_map/ppermute | solution.py:180
Sparse Core Ops, SparseCore 0:
  147.8 29.2 reduce-scatter.1
